TPU v7x, 512 devices: a whole 4x8x8 slice. The times are simulated.
512 devices in a mesh: gx: 32 (over x, z), gy: 16 (over y, core).
Axes of the slice: x: 4, y: 8, z: 8, core: 2. Of those that a mesh axis runs over, the one named last changes fastest.
Arguments:
- sources: float32 [1024, 512, 192], P('gx', 'gy'), may hold values from -12 to 12
- permeability: float32 [1024, 512], P('gx', 'gy'), may hold values from 0.2 to 5
- storage: float32 [1024, 512], P('gx', 'gy'), may hold values from 0.05 to 1
- basis: float32 [8, 1024, 512], P(None, 'gx', 'gy'), may hold values from -0.3 to 0.3
- local_inverse: bfloat16 [32, 16, 1024, 1600], P('gx', 'gy'), may hold values from -0.2 to 0.4
- coarse_inverse: float32 [4096, 4096], P(('gx', 'gy')), may hold values from -1.2 to 2.2
Outputs:
- solution: float32 [1024, 512, 192], P('gx', 'gy')
- residual_norms: float32 [3, 192], replicated
- initial_norms: float32 [192], replicated
All inputs are finite; a program needn't handle non-finite values.
Results may differ from a plain program's by a relative error of at most 0.0007.
Values may be sent and summed in bfloat16 or wider, within the bound.
No kernel may reach another device: no remote copies, remote signals or barrier semaphores. Data moves between devices by JAX's collectives and lax.ppermute only.
A program may use at most 64 MiB of HBM per device.

v0:
```python
import jax
import jax.numpy as jnp
from jax import lax
from jax.sharding import PartitionSpec as P

OV = 4
ITERS = 3
lower_bound = 0.15
upper_bound = 1.9
highest = lax.Precision.HIGHEST


def extended(cells, sides, width):
    for axis, dim in sides:
        count = lax.axis_size(axis)
        ends = count - 1
        head = lax.slice_in_dim(cells, 0, width, axis=dim)
        tail = lax.slice_in_dim(cells, cells.shape[dim] - width, cells.shape[dim], axis=dim)
        cells = jnp.concatenate(
            [
                lax.ppermute(tail, axis, [(i, (i + 1) % count) for i in range(ends)]),
                cells,
                lax.ppermute(head, axis, [((i + 1) % count, i) for i in range(ends)]),
            ],
            axis=dim,
        )
    return cells


def neighbour(padded, offset_row, offset_col):
    inner_rows = padded.shape[0] - 2
    inner_cols = padded.shape[1] - 2
    return padded[
        1 + offset_row : 1 + offset_row + inner_rows, 1 + offset_col : 1 + offset_col + inner_cols
    ]


def operate(field_pad, kappa_pad, storage_used):
    centre = neighbour(field_pad, 0, 0)
    kappa = neighbour(kappa_pad, 0, 0)
    total = storage_used[:, :, None] * centre
    for offset_row, offset_col in ((1, 0), (-1, 0), (0, 1), (0, -1)):
        faces = 0.5 * (kappa + neighbour(kappa_pad, offset_row, offset_col))
        total = total + faces[:, :, None] * (centre - neighbour(field_pad, offset_row, offset_col))
    return total


def on_device(sources, permeability, storage, basis, local_inverse, coarse_inverse):
    patch = sources.shape[0]
    fields = sources.shape[2]
    modes = basis.shape[0]
    margin = OV
    extent = patch + 2 * margin
    cells = float(patch * patch * lax.axis_size("gx") * lax.axis_size("gy"))
    flat_basis = basis.reshape(modes, patch * patch)
    inverse_rows = local_inverse[0, 0]
    stacked = jnp.stack([permeability, storage])
    padded = extended(stacked, (("gx", 1), ("gy", 2)), 1)
    kappa_pad = padded[0]
    state = sources

    def rounded_window(current):
        return extended(current.astype(jnp.bfloat16), (("gx", 0), ("gy", 1)), margin)

    def squares_total(current_core):
        return lax.psum(jnp.sum(current_core * current_core, axis=(0, 1)), ("gx", "gy"))

    def precondition(current):
        window = rounded_window(current).reshape(extent * extent, fields)
        local_part = jnp.dot(inverse_rows, window, preferred_element_type=jnp.float32).reshape(
            patch, patch, fields
        )
        flat_core = current.reshape(patch * patch, fields)
        restricted = jnp.dot(flat_basis, flat_core, precision=highest)
        coarse_part = jnp.dot(
            coarse_inverse,
            lax.all_gather(restricted, ("gx", "gy"), axis=0, tiled=True),
            precision=highest,
        )
        squares = squares_total(current)
        prolonged = jnp.dot(flat_basis.T, coarse_part, precision=highest).reshape(
            patch, patch, fields
        )
        return (local_part + prolonged, squares)

    centre = 0.5 * (upper_bound + lower_bound)
    half_width = 0.5 * (upper_bound - lower_bound)
    relative = centre / half_width
    weight_prev = 1.0 / relative
    solution = jnp.zeros_like(sources)
    corrected, initial = precondition(state)
    history = []
    update = corrected / centre
    for index in range(ITERS):
        solution = solution + update
        step_pad = extended(update, (("gx", 0), ("gy", 1)), 1)
        state = state - operate(step_pad, kappa_pad, storage)
        if index + 1 < ITERS:
            corrected, squares = precondition(state)
            history.append(squares)
            weight_next = 1.0 / (2.0 * relative - weight_prev)
            update = weight_next * weight_prev * update + 2.0 * weight_next / half_width * corrected
            weight_prev = weight_next
        else:
            history.append(squares_total(state))
    return (solution, jnp.sqrt(jnp.stack(history) / cells), jnp.sqrt(initial / cells))


def solution(mesh):
    placed = (
        P("gx", "gy", None),
        P("gx", "gy"),
        P("gx", "gy"),
        P(None, "gx", "gy"),
        P("gx", "gy", None, None),
        P(("gx", "gy"), None),
    )
    return jax.shard_map(
        on_device,
        mesh=mesh,
        in_specs=placed,
        out_specs=(P("gx", "gy", None), P(), P()),
        check_vma=False,
    )
```

profile of v0, /device:TPU:1, one launch (start us, length us, event | category | flops | bytes accessed | tf_op | source)
XLA Modules:
  0.0 572.1 jit_solution(11102322538769110874)
XLA Ops:
  11.5 5.4 collective-permute-start.4
  22.0 4.7 collective-permute-start
  33.1 5.6 collective-permute-start.2
  41.9 3.1 collective-permute-start.6
  49.4 86.9 %all-gather.4.cloned.1.call-done = f32[4096,192]{1,0:T(8,128)} async-done(((f32[8,192]{1,0:T(8,128)}), f32[4096,192]{1,0:T(8,128)}) %all-gather.4.cloned.1.call-update) | async-done | bytes 3145744 | tf_op jit(solution)/shard_map/all_gather | solution.py:77
  136.3 4.3 fusion.90
  154.7 3.6 collective-permute-start.10
  172.5 4.0 collective-permute-done.13
  176.5 5.0 collective-permute-start.14
  183.7 4.0 collective-permute-done.15
  189.1 96.9 %all-gather.6.cloned.1.call-done = f32[4096,192]{1,0:T(8,128)} async-done(((f32[8,192]{1,0:T(8,128)}), f32[4096,192]{1,0:T(8,128)}) %all-gather.6.cloned.1.call-update) | async-done | bytes 3145744 | tf_op jit(solution)/shard_map/all_gather | solution.py:77
  285.9 4.3 fusion.92
  301.2 3.3 collective-permute-done.16
  304.6 3.6 collective-permute-start.18
  317.3 3.1 collective-permute-start.20
  322.1 3.9 collective-permute-done.21
  327.0 5.1 collective-permute-start.22
  334.1 4.0 collective-permute-done.23
  340.4 95.6 %all-gather.8.cloned.1.call-done = f32[4096,192]{1,0:T(8,128)} async-done(((f32[8,192]{1,0:T(8,128)}), f32[4096,192]{1,0:T(8,128)}) %all-gather.8.cloned.1.call-update) | async-done | bytes 3145744 | tf_op jit(solution)/shard_map/all_gather | solution.py:77
  436.0 4.3 fusion.94
  445.4 3.3 multiply_add_fusion
  452.9 3.3 collective-permute-done.24
  456.3 3.6 collective-permute-start.26
  465.3 99.0 %all-reduce = (f32[1,192]{1,0:T(1,128)S(1)}, f32[1,192]{1,0:T(1,128)S(1)}, f32[1,192]{1,0:T(1,128)S(1)}, f32[192]{0:T(256)S(1)}) all-reduce(f32[1,192]{1,0:T(1,128)S(1)} %bitcast.86, f32[1,192]{1,0:T(1,128)S(1)} %bitcast.85, f32[1,192]{1,0:T(1,128)S(1)} %bitcast.87, f32[192]{0:T(256)S(1)} %copy-done.32), channel_id=1, replica_groups=mesh['gx'=32,'gy'=16] {'gx','gy'}, use_global_device_ids=true, to_apply=%region_5.0 | all-reduce | flops 768 | bytes 6144 | tf_op jit(solution)/shard_map/psum | solution.py:66
  (157 shorter events, 97.7 us)
Async XLA Ops:
  7.2 129.1 %all-gather.4.cloned.1.call-start = ((), (), s32[]{:S(2)}) async-start(), calls=%async_computation | async-start | bytes 4202496 | tf_op jit(solution)/shard_map/all_gather | solution.py:77
  10.1 275.8 %all-gather.6.cloned.1.call-start = ((), (), s32[]{:S(2)}) async-start(), calls=%async_computation.1 | async-start | bytes 4202496 | tf_op jit(solution)/shard_map/all_gather | solution.py:77
  11.5 17.8 %collective-permute-start.4 = (f32[2,1,32]{2,1,0:T(1,128)}, f32[2,1,32]{2,1,0:T(1,128)}, u32[]{:S(2)}, u32[]{:S(2)}) collective-permute-start(f32[2,1,32]{2,1,0:T(1,128)} %get-tuple-element.43), channel_id=1, source_target_pairs={{0,16},{16,32},{32,48},{48,64},{64,80},{80,96},{96,112},{112,128},... | collective-permute-start | bytes 776 | tf_op jit(solution)/shard_map/ppermute | solution.py:21
  16.8 12.5 %collective-permute-start.5 = (f32[2,1,32]{2,1,0:T(1,128)}, f32[2,1,32]{2,1,0:T(1,128)}, u32[]{:S(2)}, u32[]{:S(2)}) collective-permute-start(f32[2,1,32]{2,1,0:T(1,128)} %get-tuple-element.44), channel_id=1, source_target_pairs={{16,0},{32,16},{48,32},{64,48},{80,64},{96,80},{112,96},{128,112},... | collective-permute-start | bytes 776 | tf_op jit(solution)/shard_map/ppermute | solution.py:23
  22.0 8.1 %collective-permute-start = (bf16[4,32,192]{2,1,0:T(8,128)(2,1)}, bf16[4,32,192]{2,1,0:T(8,128)(2,1)}, u32[]{:S(2)}, u32[]{:S(2)}) collective-permute-start(bf16[4,32,192]{2,1,0:T(8,128)(2,1)} %get-tuple-element.39), channel_id=1, source_target_pairs={{0,16},{16,32},{32,48},{48,64},{64,80},{80,96},{96,112},{112,128},... | collective-permute-start | bytes 147464 | tf_op jit(solution)/shard_map/ppermute | solution.py:21
  26.7 5.3 collective-permute-start.1
  33.1 13.8 %collective-permute-start.2 = (bf16[40,4,192]{2,1,0:T(4,128)(2,1)S(1)}, bf16[40,4,192]{2,1,0:T(4,128)(2,1)S(1)}, u32[]{:S(2)}, u32[]{:S(2)}) collective-permute-start(bf16[40,4,192]{2,1,0:T(4,128)(2,1)S(1)} %get-tuple-element.33), channel_id=1, source_target_pairs={{0,1},{1,2},{2,3},{3,4},{4,5},{5,6},{6,7},{7,8},{8,9},{9,10},{10,1... | collective-permute-start | bytes 184328 | tf_op jit(solution)/shard_map/ppermute | solution.py:21
  38.7 8.2 %collective-permute-start.3 = (bf16[40,4,192]{2,1,0:T(4,128)(2,1)S(1)}, bf16[40,4,192]{2,1,0:T(4,128)(2,1)S(1)}, u32[]{:S(2)}, u32[]{:S(2)}) collective-permute-start(bf16[40,4,192]{2,1,0:T(4,128)(2,1)S(1)} %get-tuple-element.34), channel_id=1, source_target_pairs={{1,0},{2,1},{3,2},{4,3},{5,4},{6,5},{7,6},{8,7},{9,8},{10,9},{11,1... | collective-permute-start | bytes 184328 | tf_op jit(solution)/shard_map/ppermute | solution.py:23
  41.9 109.3 %collective-permute-start.6 = (f32[2,34,1]{2,1,0:T(8,128)}, f32[2,34,1]{2,1,0:T(8,128)}, u32[]{:S(2)}, u32[]{:S(2)}) collective-permute-start(f32[2,34,1]{2,1,0:T(8,128)} %get-tuple-element.41), channel_id=1, source_target_pairs={{0,1},{1,2},{2,3},{3,4},{4,5},{5,6},{6,7},{7,8},{8,9},{9,10},{10,1... | collective-permute-start | bytes 824 | tf_op jit(solution)/shard_map/ppermute | solution.py:21
  45.0 106.2 %collective-permute-start.7 = (f32[2,34,1]{2,1,0:T(8,128)}, f32[2,34,1]{2,1,0:T(8,128)}, u32[]{:S(2)}, u32[]{:S(2)}) collective-permute-start(f32[2,34,1]{2,1,0:T(8,128)} %get-tuple-element.42), channel_id=1, source_target_pairs={{1,0},{2,1},{3,2},{4,3},{5,4},{6,5},{7,6},{8,7},{9,8},{10,9},{11,1... | collective-permute-start | bytes 824 | tf_op jit(solution)/shard_map/ppermute | solution.py:23
  147.2 4.9 collective-permute-start.9
  154.7 6.0 %collective-permute-start.10 = (f32[34,1,192]{2,1,0:T(1,128)S(1)}, f32[34,1,192]{2,1,0:T(1,128)S(1)}, u32[]{:S(2)}, u32[]{:S(2)}) collective-permute-start(f32[34,1,192]{2,1,0:T(1,128)S(1)} %get-tuple-element.19), channel_id=1, source_target_pairs={{1,0},{2,1},{3,2},{4,3},{5,4},{6,5},{7,6},{8,7},{9,8},{10,9},{11,1... | collective-permute-start | bytes 78344 | tf_op jit(solution)/shard_map/ppermute | solution.py:23
  166.4 269.6 %all-gather.8.cloned.1.call-start = ((), (), s32[]{:S(2)}) async-start(), calls=%async_computation.2 | async-start | bytes 4202496 | tf_op jit(solution)/shard_map/all_gather | solution.py:77
  167.7 4.7 collective-permute-start.12
  170.8 5.6 collective-permute-start.13
  176.5 7.2 %collective-permute-start.14 = (bf16[40,4,192]{2,1,0:T(4,128)(2,1)S(1)}, bf16[40,4,192]{2,1,0:T(4,128)(2,1)S(1)}, u32[]{:S(2)}, u32[]{:S(2)}) collective-permute-start(bf16[40,4,192]{2,1,0:T(4,128)(2,1)S(1)} %get-tuple-element.31), channel_id=1, source_target_pairs={{0,1},{1,2},{2,3},{3,4},{4,5},{5,6},{6,7},{7,8},{8,9},{9,10},{10,1... | collective-permute-start | bytes 184328 | tf_op jit(solution)/shard_map/ppermute | solution.py:21
  181.6 6.2 %collective-permute-start.15 = (bf16[40,4,192]{2,1,0:T(4,128)(2,1)S(1)}, bf16[40,4,192]{2,1,0:T(4,128)(2,1)S(1)}, u32[]{:S(2)}, u32[]{:S(2)}) collective-permute-start(bf16[40,4,192]{2,1,0:T(4,128)(2,1)S(1)} %get-tuple-element.32), channel_id=1, source_target_pairs={{1,0},{2,1},{3,2},{4,3},{5,4},{6,5},{7,6},{8,7},{9,8},{10,9},{11,1... | collective-permute-start | bytes 184328 | tf_op jit(solution)/shard_map/ppermute | solution.py:23
  299.9 4.7 collective-permute-start.16
  304.6 5.9 %collective-permute-start.18 = (f32[34,1,192]{2,1,0:T(1,128)S(1)}, f32[34,1,192]{2,1,0:T(1,128)S(1)}, u32[]{:S(2)}, u32[]{:S(2)}) collective-permute-start(f32[34,1,192]{2,1,0:T(1,128)S(1)} %get-tuple-element.17), channel_id=1, source_target_pairs={{1,0},{2,1},{3,2},{4,3},{5,4},{6,5},{7,6},{8,7},{9,8},{10,9},{11,1... | collective-permute-start | bytes 78344 | tf_op jit(solution)/shard_map/ppermute | solution.py:23
  317.3 4.8 collective-permute-start.20
  320.4 5.6 collective-permute-start.21
  327.0 7.0 %collective-permute-start.22 = (bf16[40,4,192]{2,1,0:T(4,128)(2,1)S(1)}, bf16[40,4,192]{2,1,0:T(4,128)(2,1)S(1)}, u32[]{:S(2)}, u32[]{:S(2)}) collective-permute-start(bf16[40,4,192]{2,1,0:T(4,128)(2,1)S(1)} %get-tuple-element.29), channel_id=1, source_target_pairs={{0,1},{1,2},{2,3},{3,4},{4,5},{5,6},{6,7},{7,8},{8,9},{9,10},{10,1... | collective-permute-start | bytes 184328 | tf_op jit(solution)/shard_map/ppermute | solution.py:21
  332.1 5.9 %collective-permute-start.23 = (bf16[40,4,192]{2,1,0:T(4,128)(2,1)S(1)}, bf16[40,4,192]{2,1,0:T(4,128)(2,1)S(1)}, u32[]{:S(2)}, u32[]{:S(2)}) collective-permute-start(bf16[40,4,192]{2,1,0:T(4,128)(2,1)S(1)} %get-tuple-element.30), channel_id=1, source_target_pairs={{1,0},{2,1},{3,2},{4,3},{5,4},{6,5},{7,6},{8,7},{9,8},{10,9},{11,1... | collective-permute-start | bytes 184328 | tf_op jit(solution)/shard_map/ppermute | solution.py:23
  456.3 5.9 %collective-permute-start.26 = (f32[34,1,192]{2,1,0:T(1,128)S(1)}, f32[34,1,192]{2,1,0:T(1,128)S(1)}, u32[]{:S(2)}, u32[]{:S(2)}) collective-permute-start(f32[34,1,192]{2,1,0:T(1,128)S(1)} %get-tuple-element.15), channel_id=1, source_target_pairs={{1,0},{2,1},{3,2},{4,3},{5,4},{6,5},{7,6},{8,7},{9,8},{10,9},{11,1... | collective-permute-start | bytes 78344 | tf_op jit(solution)/shard_map/ppermute | solution.py:23
  (41 other events, 724.6 us)
Sparse Core Ops, SparseCore 0:
  12.2 124.0 all-gather.3
  166.5 119.3 all-gather.5
  316.6 119.3 all-gather.7
where the time goes:
time: 574 us; the launch traced here: 572 us
  waiting for transfers between devices  310 us (54%)
  blocking collectives  99 us (17%)
  starting transfers between devices  78.5 us (14%)
  other arithmetic  30.5 us (5%)
  matrix products  26.2 us (5%)
  between operations  14.4 us (3%)
  local copies, waits for them, and re-layouts  13.3 us (2%)
    all_gather x3, waiting for transfers between devices, precondition(): lax.all_gather(restricted, ('gx', 'gy'), axis=0, tiled=True)  279 us
    psum x1, blocking collectives, squares_total(): lax.psum(jnp.sum(current_core * current_core, axis=(0, 1)), ('gx', 'gy'))  99 us
    ppermute x14, starting transfers between devices, extended(): lax.ppermute(tail, axis, [(i, (i + 1) % count) for i in range(ends)])  50.1 us
    ppermute x14, starting transfers between devices, extended(): lax.ppermute(head, axis, [((i + 1) % count, i) for i in range(ends)])  28.3 us
    ppermute x14, waiting for transfers between devices, extended(): lax.ppermute(head, axis, [((i + 1) % count, i) for i in range(ends)])  27 us
    dot_general x3, matrix products, precondition(): jnp.dot(coarse_inverse, lax.all_gather(restricted, ('gx', 'gy'), axis=0,...  12.9 us
  transfers between devices with their start and end apart: 31, of which 16 were waited for; matrix products, arithmetic and copies ran while one was open for 5% of the time, Pallas kernels for 0%

commit v1 on v0

--- a/solution.py
+++ b/solution.py
@@ -63,7 +63,9 @@
         return extended(current.astype(jnp.bfloat16), (("gx", 0), ("gy", 1)), margin)
 
     def squares_total(current_core):
-        return lax.psum(jnp.sum(current_core * current_core, axis=(0, 1)), ("gx", "gy"))
+        return jnp.sum(
+            lax.all_gather(jnp.sum(current_core * current_core, axis=(0, 1)), ("gx", "gy")), axis=0
+        )
 
     def precondition(current):
         window = rounded_window(current).reshape(extent * extent, fields)

time: 574 us -> 781 us (1.36)
  waiting for transfers between devices: 310 us -> 584 us
  blocking collectives: 99 us -> 0 us
  local copies, waits for them, and re-layouts: 13.3 us -> 29.9 us
  starting transfers between devices: 78.5 us -> 87.2 us
    unnamed x3 -> x5, waiting for transfers between devices: 0.05 us -> 282 us
    psum x1 -> x0, blocking collectives: 99 us -> none  [squares_total(): lax.psum(jnp.sum(current_core * current_core, axis=(0, 1)), ('gx', 'gy'))]
    ppermute x14, waiting for transfers between devices: 27 us -> 6.71 us  [extended(): lax.ppermute(head, axis, [((i + 1) % count, i) for i in range(ends)])]
    unnamed x68 -> x78, local copies, waits for them, and re-layouts: 2.93 us -> 11.7 us
    all_gather x3, waiting for transfers between devices: 279 us -> 288 us  [precondition(): lax.all_gather(restricted, ('gx', 'gy'), axis=0, tiled=True)]
  transfers between devices with their start and end apart: 31 -> 32, of which waited for: 16 -> 14; matrix products, arithmetic and copies ran while one was open for 5% -> 4% of each run, Pallas kernels for 0% -> 0%
where the time goes in v1:
time: 781 us; the launch traced here: 779 us
  waiting for transfers between devices  584 us (75%)
  starting transfers between devices  87.2 us (11%)
  other arithmetic  37.1 us (5%)
  local copies, waits for them, and re-layouts  29.9 us (4%)
  matrix products  26.1 us (3%)
  between operations  14.5 us (2%)
    all_gather x3, waiting for transfers between devices, precondition(): lax.all_gather(restricted, ('gx', 'gy'), axis=0, tiled=True)  288 us
    unnamed x5, waiting for transfers between devices  282 us
    ppermute x14, starting transfers between devices, extended(): lax.ppermute(tail, axis, [(i, (i + 1) % count) for i in range(ends)])  57.3 us
    ppermute x14, starting transfers between devices, extended(): lax.ppermute(head, axis, [((i + 1) % count, i) for i in range(ends)])  29.7 us
  transfers between devices with their start and end apart: 32, of which 14 were waited for; matrix products, arithmetic and copies ran while one was open for 4% of the time, Pallas kernels for 0%

profile of v1, /device:TPU:1, one launch (start us, length us, event | category | flops | bytes accessed | tf_op | source)
XLA Modules:
  0.0 778.6 jit_solution(11953575737199568472)
XLA Ops:
  15.3 6.1 collective-permute-start
  23.2 4.6 collective-permute-start.4
  30.9 8.4 %collective-permute-start.3 = (bf16[40,4,192]{2,1,0:T(4,128)(2,1)S(1)}, bf16[40,4,192]{2,1,0:T(4,128)(2,1)S(1)}, u32[]{:S(2)}, u32[]{:S(2)}) collective-permute-start(bf16[40,4,192]{2,1,0:T(4,128)(2,1)S(1)} %get-tuple-element.34), channel_id=1, source_target_pairs={{1,0},{2,1},{3,2},{4,3},{5,4},{6,5},{7,6},{8,7},{9,8},{10,9},{11,1... | collective-permute-start | bytes 184328 | tf_op jit(solution)/shard_map/ppermute | solution.py:23
  49.9 86.4 %all-gather.8.cloned.1.call-done = f32[4096,192]{1,0:T(8,128)} async-done(((f32[8,192]{1,0:T(8,128)}), f32[4096,192]{1,0:T(8,128)}) %all-gather.8.cloned.1.call-update) | async-done | bytes 3145744 | tf_op jit(solution)/shard_map/all_gather | solution.py:79
  136.3 4.3 fusion.90
  148.5 4.0 collective-permute-start.9
  153.6 4.3 collective-permute-start.11
  160.0 3.2 collective-permute-done.10
  170.6 4.6 collective-permute-start.12
  178.5 3.8 collective-permute-start.14
  185.0 101.6 %all-gather.10.cloned.1.call-done = f32[4096,192]{1,0:T(8,128)} async-done(((f32[8,192]{1,0:T(8,128)}), f32[4096,192]{1,0:T(8,128)}) %all-gather.10.cloned.1.call-update) | async-done | bytes 3145744 | tf_op jit(solution)/shard_map/all_gather | solution.py:79
  286.5 4.3 fusion.92
  299.1 4.0 collective-permute-start.17
  304.2 4.3 collective-permute-start.19
  310.5 3.3 collective-permute-done.18
  320.9 4.6 collective-permute-start.20
  329.8 3.6 collective-permute-start.22
  337.3 100.0 %all-gather.12.cloned.1.call-done = f32[4096,192]{1,0:T(8,128)} async-done(((f32[8,192]{1,0:T(8,128)}), f32[4096,192]{1,0:T(8,128)}) %all-gather.12.cloned.1.call-update) | async-done | bytes 3145744 | tf_op jit(solution)/shard_map/all_gather | solution.py:79
  437.3 4.3 fusion.94
  446.7 3.3 multiply_add_fusion
  451.4 4.0 collective-permute-start.25
  456.5 4.3 collective-permute-start.27
  467.5 4.9 multiply_reduce_fusion.1
  476.9 281.8 %all-reduce.7.cloned.1.call-done = (f32[98304]{0:T(1024)}, f32[98304]{0:T(1024)}, f32[98304]{0:T(1024)}, f32[98304]{0:T(1024)}) async-done(((f32[98304]{0:T(1024)}, f32[98304]{0:T(1024)}, f32[98304]{0:T(1024)}, f32[98304]{0:T(1024)}), (f32[98304]{0:T(1024)}, f32[98304]{0:T(1024)}, f32[98304]{0:T(1024)}, f32[98304]{0:T(1024)})) %all-reduce.7.cloned.1.call-update) | async-done | bytes 1572880
  (177 shorter events, 106.3 us)
Async XLA Ops:
  7.2 129.1 %all-gather.8.cloned.1.call-start = ((), (), s32[]{:S(2)}) async-start(), calls=%async_computation | async-start | bytes 4202496 | tf_op jit(solution)/shard_map/all_gather | solution.py:79
  10.1 276.5 %all-gather.10.cloned.1.call-start = ((), (), s32[]{:S(2)}) async-start(), calls=%async_computation.1 | async-start | bytes 4202496 | tf_op jit(solution)/shard_map/all_gather | solution.py:79
  14.0 15.9 %collective-permute-start.1 = (bf16[4,32,192]{2,1,0:T(8,128)(2,1)}, bf16[4,32,192]{2,1,0:T(8,128)(2,1)}, u32[]{:S(2)}, u32[]{:S(2)}) collective-permute-start(bf16[4,32,192]{2,1,0:T(8,128)(2,1)} %get-tuple-element.40), channel_id=1, source_target_pairs={{16,0},{32,16},{48,32},{64,48},{80,64},{96,80},{112,96},{128,112},... | collective-permute-start | bytes 147464 | tf_op jit(solution)/shard_map/ppermute | solution.py:23
  15.3 14.6 %collective-permute-start = (bf16[4,32,192]{2,1,0:T(8,128)(2,1)}, bf16[4,32,192]{2,1,0:T(8,128)(2,1)}, u32[]{:S(2)}, u32[]{:S(2)}) collective-permute-start(bf16[4,32,192]{2,1,0:T(8,128)(2,1)} %get-tuple-element.39), channel_id=1, source_target_pairs={{0,16},{16,32},{32,48},{48,64},{64,80},{80,96},{96,112},{112,128},... | collective-permute-start | bytes 147464 | tf_op jit(solution)/shard_map/ppermute | solution.py:21
  21.9 7.2 collective-permute-start.5
  23.2 5.9 collective-permute-start.4
  30.9 16.6 %collective-permute-start.3 = (bf16[40,4,192]{2,1,0:T(4,128)(2,1)S(1)}, bf16[40,4,192]{2,1,0:T(4,128)(2,1)S(1)}, u32[]{:S(2)}, u32[]{:S(2)}) collective-permute-start(bf16[40,4,192]{2,1,0:T(4,128)(2,1)S(1)} %get-tuple-element.34), channel_id=1, source_target_pairs={{1,0},{2,1},{3,2},{4,3},{5,4},{6,5},{7,6},{8,7},{9,8},{10,9},{11,1... | collective-permute-start | bytes 184328 | tf_op jit(solution)/shard_map/ppermute | solution.py:23
  39.3 8.2 %collective-permute-start.2 = (bf16[40,4,192]{2,1,0:T(4,128)(2,1)S(1)}, bf16[40,4,192]{2,1,0:T(4,128)(2,1)S(1)}, u32[]{:S(2)}, u32[]{:S(2)}) collective-permute-start(bf16[40,4,192]{2,1,0:T(4,128)(2,1)S(1)} %get-tuple-element.33), channel_id=1, source_target_pairs={{0,1},{1,2},{2,3},{3,4},{4,5},{5,6},{6,7},{7,8},{8,9},{9,10},{10,1... | collective-permute-start | bytes 184328 | tf_op jit(solution)/shard_map/ppermute | solution.py:21
  41.9 110.6 %collective-permute-start.7 = (f32[2,34,1]{2,1,0:T(8,128)}, f32[2,34,1]{2,1,0:T(8,128)}, u32[]{:S(2)}, u32[]{:S(2)}) collective-permute-start(f32[2,34,1]{2,1,0:T(8,128)} %get-tuple-element.42), channel_id=1, source_target_pairs={{1,0},{2,1},{3,2},{4,3},{5,4},{6,5},{7,6},{8,7},{9,8},{10,9},{11,1... | collective-permute-start | bytes 824 | tf_op jit(solution)/shard_map/ppermute | solution.py:23
  44.3 108.2 %collective-permute-start.6 = (f32[2,34,1]{2,1,0:T(8,128)}, f32[2,34,1]{2,1,0:T(8,128)}, u32[]{:S(2)}, u32[]{:S(2)}) collective-permute-start(f32[2,34,1]{2,1,0:T(8,128)} %get-tuple-element.41), channel_id=1, source_target_pairs={{0,1},{1,2},{2,3},{3,4},{4,5},{5,6},{6,7},{7,8},{8,9},{9,10},{10,1... | collective-permute-start | bytes 824 | tf_op jit(solution)/shard_map/ppermute | solution.py:21
  147.2 6.2 collective-permute-start.8
  153.6 6.4 collective-permute-start.11
  168.0 269.3 %all-gather.12.cloned.1.call-start = ((), (), s32[]{:S(2)}) async-start(), calls=%async_computation.2 | async-start | bytes 4202496 | tf_op jit(solution)/shard_map/all_gather | solution.py:79
  169.3 5.9 collective-permute-start.13
  170.6 5.9 collective-permute-start.12
  176.6 5.8 collective-permute-start.15
  304.2 6.3 collective-permute-start.19
  318.7 439.9 %all-reduce.7.cloned.1.call-start = ((), (), s32[]{:S(2)}) async-start(), calls=%async_computation.3 | async-start | bytes 3145728
  319.6 5.9 collective-permute-start.21
  320.9 5.9 collective-permute-start.20
  327.9 5.8 collective-permute-start.23
  450.0 5.4 collective-permute-start.24
  456.5 10.9 %collective-permute-start.27 = (f32[34,1,192]{2,1,0:T(1,128)S(1)}, f32[34,1,192]{2,1,0:T(1,128)S(1)}, u32[]{:S(2)}, u32[]{:S(2)}) collective-permute-start(f32[34,1,192]{2,1,0:T(1,128)S(1)} %get-tuple-element.16), channel_id=1, source_target_pairs={{0,1},{1,2},{2,3},{3,4},{4,5},{5,6},{6,7},{7,8},{8,9},{9,10},{10,1... | collective-permute-start | bytes 78344 | tf_op jit(solution)/shard_map/ppermute | solution.py:21
  460.8 6.6 collective-permute-start.26
  (43 other events, 772.8 us)
Sparse Core Ops, SparseCore 0:
  12.2 124.0 all-gather.7
  168.1 118.4 all-gather.9
  318.8 118.4 all-gather.11
  477.0 281.5 all-reduce.6
